TPU v7x, 512 devices: a whole 4x4x16 slice. The times are simulated.
512 devices in a mesh: tok: 64 (over z, x), head: 8 (over y, core).
Axes of the slice: x: 4, y: 4, z: 16, core: 2. Of those that a mesh axis runs over, the one named last changes fastest.
Arguments:
- tokens: bfloat16 [32768, 2560], P('tok', 'head'), may hold values from -6 to 6
- query_weight: bfloat16 [2560, 2560], P('tok'), may hold values from -0.125 to 0.125
- keyvalue_weight: bfloat16 [2560, 512], P('tok'), may hold values from -0.125 to 0.125
- output_weight: bfloat16 [2560, 2560], P(None, ('head', 'tok')), may hold values from -0.125 to 0.125
- cache: bfloat16 [2048, 2, 128, 256], P(('tok', 'head')), may hold values from -460 to 460
- page_table: int32 [512, 4], P('tok'), may hold values from 0 to 2047, as said below
- parents: int32 [512, 64], P('tok'), may hold values from 0 to 62, as said below
- cache_len: int32 [512], P('tok'), may hold values from 1 to 448, as said below
- accepted_leaf: int32 [512], P('tok'), may hold values from 0 to 63
Outputs:
- attended: bfloat16 [32768, 2560], P('tok', 'head')
- cache_out: bfloat16 [2048, 2, 128, 256], P(('tok', 'head'))
Inputs may be any that keep to these rules, and one draw needn't show every extreme that they name: `page_table`: for every d, row d names each of the pages d * 4 to d * 4 + 3 exactly once, so request d's pages all lie on device d (devices counted tok-major, head-minor). parents[r, 0] = 0, and parents[r, i] < i for i >= 1. `cache_len`: roughly half of the requests hold at most 128 cached positions, the others more than 320.
All inputs are finite; a program needn't handle non-finite values.
Results may differ from a plain program's by a relative error of at most 0.014.
The roundings to bfloat16 on the way count: a program that leaves them out, or rounds other values in their place, can miss the bound.
Values may be sent and summed in bfloat16 or wider, within the bound.
No kernel may reach another device: no remote copies, remote signals or barrier semaphores. Data moves between devices by JAX's collectives and lax.ppermute only.
A program may use at most 64 MiB of HBM per device.

v0:
```python
import math
import jax
import jax.numpy as jnp
from jax import lax
from jax.sharding import PartitionSpec as P

HQ = 10
HD = 256
DRAFT = 64
PAGE = 128
NPR = 4
WINDOW = 256


def ancestry(parent_row):
    node_ids = jnp.arange(DRAFT, dtype=jnp.int32)
    link = (parent_row[:, None] == node_ids[None, :]).astype(jnp.float32)
    reach = jnp.minimum(link + jnp.eye(DRAFT, dtype=jnp.float32), 1.0)
    for sweep in range((DRAFT - 1).bit_length()):
        reach = jnp.minimum(jnp.dot(reach, reach, precision=lax.Precision.HIGHEST), 1.0)
    depth = (jnp.sum(reach, axis=1) - 1.0).astype(jnp.int32)
    return (reach, depth)


def rotate(values, position):
    half = HD // 4
    freq = jnp.exp(jnp.arange(half, dtype=jnp.float32) * (-2.0 * math.log(10000.0) / (HD // 2)))
    angle = position.astype(jnp.float32)[..., None] * freq
    cosine = jnp.cos(angle)
    sine = jnp.sin(angle)
    first = values[..., :half]
    second = values[..., half : 2 * half]
    return jnp.concatenate(
        [first * cosine - second * sine, second * cosine + first * sine, values[..., 2 * half :]],
        axis=-1,
    )


def attend(queries, cache_keys, cache_values, tree_keys, tree_values, lengths, position, reach):
    window_span = cache_keys.shape[1]
    slot_ids = jnp.arange(window_span, dtype=jnp.int32)
    visible = (slot_ids[None, None, :] < lengths[:, None, None]) & (
        slot_ids[None, None, :] > position[:, :, None] - WINDOW
    )
    cache_scores = jnp.einsum(
        "rnhd,rcd->rhnc", queries, cache_keys, preferred_element_type=jnp.float32
    )
    tree_scores = jnp.einsum(
        "rnhd,rmd->rhnm", queries, tree_keys, preferred_element_type=jnp.float32
    )
    cache_scores = jnp.where(visible[:, None], cache_scores, -1e30)
    tree_scores = jnp.where(reach[:, None] > 0.5, tree_scores, -1e30)
    row_peak = jnp.maximum(jnp.max(cache_scores, axis=-1), jnp.max(tree_scores, axis=-1))[..., None]
    cache_weights = jnp.exp(cache_scores - row_peak)
    tree_weights = jnp.exp(tree_scores - row_peak)
    denominator = jnp.sum(cache_weights, axis=-1, keepdims=True) + jnp.sum(
        tree_weights, axis=-1, keepdims=True
    )
    cache_weights = (cache_weights / denominator).astype(jnp.bfloat16)
    tree_weights = (tree_weights / denominator).astype(jnp.bfloat16)
    result = jnp.einsum(
        "rhnc,rcd->rnhd", cache_weights, cache_values, preferred_element_type=jnp.float32
    )
    result = result + jnp.einsum(
        "rhnm,rmd->rnhd", tree_weights, tree_values, preferred_element_type=jnp.float32
    )
    return result.astype(jnp.bfloat16)


def refresh(logical_pages, length, leaf, reach, depth, new_keys, new_values):
    count = logical_pages.shape[0] * logical_pages.shape[2]
    logical = jnp.transpose(logical_pages, (1, 0, 2, 3)).reshape(2, count, HD)
    slot_ids = jnp.arange(count, dtype=jnp.int32)
    on_path = reach[leaf]
    selector = ((on_path[None, :] > 0.5) & (depth[None, :] == slot_ids[:, None] - length)).astype(
        jnp.float32
    )
    placed_keys = jnp.dot(selector, new_keys.astype(jnp.float32), precision=lax.Precision.HIGHEST)
    placed_values = jnp.dot(
        selector, new_values.astype(jnp.float32), precision=lax.Precision.HIGHEST
    )
    placed = jnp.stack([placed_keys, placed_values]).astype(jnp.bfloat16)
    written = jnp.sum(selector, axis=1) > 0.5
    logical = jnp.where(written[None, :, None], placed, logical)
    return jnp.transpose(
        logical.reshape(2, logical_pages.shape[0], logical_pages.shape[2], HD), (1, 0, 2, 3)
    )


def contract(source, piece):
    return jnp.dot(source, piece, preferred_element_type=jnp.float32)


def project_memory(rows, keyvalue_weight, position):
    projected = contract(rows, lax.all_gather(keyvalue_weight, "tok", axis=0, tiled=True))
    new_keys = rotate(projected[:, :HD], position).astype(jnp.bfloat16)
    new_values = projected[:, HD:].astype(jnp.bfloat16)
    return (new_keys, new_values)


def split_pages(page_blocks, count):
    cache_keys = page_blocks[:, :, 0].reshape(count, NPR * PAGE, HD)
    cache_values = page_blocks[:, :, 1].reshape(count, NPR * PAGE, HD)
    return (cache_keys, cache_values)


def reduce_heads(mixed, output_weight, safe_heads, head_mask, slots_per):
    head_count = lax.axis_size("head")
    tok_count = lax.axis_size("tok")
    narrow = output_weight.shape[1]
    blocks = lax.all_gather(output_weight, "head", axis=1, tiled=True)
    part_cols = blocks.shape[1]
    my_output_weight = (
        jnp.take(blocks.reshape(HQ, HD, part_cols), safe_heads, axis=0) * head_mask[:, None, None]
    )
    my_output_weight = my_output_weight.reshape(slots_per * HD, part_cols)
    partial_value = jnp.dot(
        mixed,
        lax.all_gather(my_output_weight, "tok", axis=1, tiled=True),
        preferred_element_type=jnp.float32,
    ).astype(jnp.bfloat16)
    row_count = partial_value.shape[0]
    partial_value = partial_value.reshape(row_count, tok_count, head_count, narrow)
    partial_value = jnp.transpose(partial_value, (0, 2, 1, 3)).reshape(
        row_count, tok_count * head_count * narrow
    )
    partial_value = lax.optimization_barrier(partial_value)
    summed = lax.psum_scatter(
        partial_value.astype(jnp.float32).astype(jnp.bfloat16),
        "head",
        scatter_dimension=1,
        tiled=True,
    )
    return summed


def shards(
    tokens,
    query_weight,
    keyvalue_weight,
    output_weight,
    cache,
    page_table,
    parents,
    cache_len,
    accepted_leaf,
):
    head_count = lax.axis_size("head")
    head_index = lax.axis_index("head")
    tok_index = lax.axis_index("tok")
    slots_per = -(-HQ // head_count)
    requests = parents.shape[0]
    owned = requests // head_count
    rows_owned = owned * DRAFT
    pages_dev = cache.shape[0]
    gathered = lax.all_gather(tokens, "head", axis=1, tiled=True)
    wide = gathered.astype(jnp.float32)
    mean_square = jnp.mean(wide * wide, axis=1, keepdims=True)
    normed = (wide * lax.rsqrt(mean_square + 1e-06)).astype(jnp.bfloat16)
    reach, depth = jax.vmap(ancestry)(parents)
    position = cache_len[:, None] + depth
    flat_pos = position.reshape(-1)
    head_ids = head_index + head_count * jnp.arange(slots_per, dtype=jnp.int32)
    usable = head_ids < HQ
    safe_heads = jnp.minimum(head_ids, HQ - 1)
    head_mask = usable.astype(jnp.bfloat16)
    part_rows = query_weight.shape[0]
    my_query_weight = (
        jnp.take(query_weight.reshape(part_rows, HQ, HD), safe_heads, axis=1)
        * head_mask[None, :, None]
    )
    my_query_weight = my_query_weight.reshape(part_rows, slots_per * HD)
    queries = contract(normed, lax.all_gather(my_query_weight, "tok", axis=0, tiled=True))
    queries = (rotate(queries.reshape(-1, slots_per, HD), flat_pos[:, None]) * HD ** (-0.5)).astype(
        jnp.bfloat16
    )
    own_start = head_index * rows_owned
    own_reach = lax.dynamic_slice_in_dim(reach, head_index * owned, owned, 0)
    own_depth = lax.dynamic_slice_in_dim(depth, head_index * owned, owned, 0)
    own_len = lax.dynamic_slice_in_dim(cache_len, head_index * owned, owned, 0)
    own_leaf = lax.dynamic_slice_in_dim(accepted_leaf, head_index * owned, owned, 0)
    device = tok_index * head_count + head_index
    own_table = (
        lax.dynamic_slice_in_dim(page_table, head_index * owned, owned, 0) - device * pages_dev
    )
    own_pages = jnp.take(cache, own_table.reshape(-1), axis=0).reshape(owned, NPR, 2, PAGE, HD)
    tree_keys, tree_values = project_memory(normed, keyvalue_weight, flat_pos)
    own_keys = lax.dynamic_slice_in_dim(tree_keys, own_start, rows_owned, 0)
    own_values = lax.dynamic_slice_in_dim(tree_values, own_start, rows_owned, 0)
    page_pool = lax.all_gather(cache, "head", axis=0, tiled=True)
    local_ids = page_table - tok_index * head_count * pages_dev
    page_blocks = jnp.take(page_pool, local_ids.reshape(-1), axis=0).reshape(
        requests, NPR, 2, PAGE, HD
    )
    cache_keys, cache_values = split_pages(page_blocks, requests)
    result = attend(
        queries.reshape(requests, DRAFT, slots_per, HD),
        cache_keys,
        cache_values,
        tree_keys.reshape(requests, DRAFT, HD),
        tree_values.reshape(requests, DRAFT, HD),
        cache_len,
        position,
        reach,
    )
    mixed = result.reshape(-1, slots_per * HD)
    attended = reduce_heads(mixed, output_weight, safe_heads, head_mask, slots_per)
    new_pages = jax.vmap(refresh)(
        own_pages,
        own_len,
        own_leaf,
        own_reach,
        own_depth,
        own_keys.reshape(owned, DRAFT, HD),
        own_values.reshape(owned, DRAFT, HD),
    )
    flat_ids = own_table.reshape(-1)
    matches = (flat_ids[:, None] == jnp.arange(pages_dev, dtype=jnp.int32)[None, :]).astype(
        jnp.int32
    )
    inverse = jnp.sum(matches * jnp.arange(pages_dev, dtype=jnp.int32)[:, None], axis=0)
    cache_out = jnp.take(new_pages.reshape(pages_dev, 2, PAGE, HD), inverse, axis=0)
    return (attended, cache_out)


def solution(mesh):
    in_specs = (
        P("tok", "head"),
        P("tok", None),
        P("tok", None),
        P(None, ("head", "tok")),
        P(("tok", "head"), None, None, None),
        P("tok", None),
        P("tok", None),
        P("tok"),
        P("tok"),
    )
    out_specs = (P("tok", "head"), P(("tok", "head"), None, None, None))
    return jax.shard_map(shards, mesh=mesh, in_specs=in_specs, out_specs=out_specs, check_vma=False)
```

profile of v0, /device:TPU:2, one launch (start us, length us, event | category | flops | bytes accessed | tf_op | source)
XLA Modules:
  0.0 582.3 jit_solution(10205464197976937876)
XLA Ops:
  7.2 0.7 all-gather.9.cloned.1.call-update
  8.0 0.7 all-gather.13.cloned.1.call-update
  8.9 0.9 copy.116
  9.9 0.6 gather_fusion.1
  10.4 0.6 select_multiply_fusion.1
  11.1 0.5 all-gather.7.cloned.1.call-update
  11.7 13.6 %all-gather = bf16[8,5,2560]{2,1,0:T(8,128)(2,1)S(1)} all-gather(bf16[1,5,2560]{2,1,0:T(8,128)(2,1)} %bitcast.138), channel_id=1, replica_groups=mesh['tok'=64,'head'=8] {'head'}, dimensions={0}, use_global_device_ids=true | all-gather | bytes 230400 | tf_op jit(solution)/shard_map/all_gather | solution.py:111
  25.5 0.6 gather_fusion.2
  26.1 0.6 select_multiply_fusion
  26.8 0.5 convolution_minimum_fusion.5
  27.7 0.4 convolution_minimum_fusion.3
  28.9 0.5 fusion.58
  29.6 0.8 copy.86
  30.6 0.6 copy.75
  31.6 16.7 %all-gather.9.cloned.1.call-done = bf16[512,2560]{0,1:T(8,128)(2,1)} async-done(((bf16[512,320]{0,1:T(8,128)(2,1)}), bf16[512,2560]{0,1:T(8,128)(2,1)}) %all-gather.9.cloned.1.call-update) | async-done | bytes 2621456 | tf_op jit(solution)/shard_map/all_gather | solution.py:156
  48.3 2.5 fusion
  50.8 141.9 %all-gather.13.cloned.1.call-done = bf16[2560,512]{1,0:T(8,128)(2,1)} async-done(((bf16[40,512]{1,0:T(8,128)(2,1)}), bf16[2560,512]{1,0:T(8,128)(2,1)}) %all-gather.13.cloned.1.call-update) | async-done | bytes 2621456 | tf_op jit(solution)/shard_map/all_gather | solution.py:95
  192.7 3.3 fusion.2
  196.0 0.7 slice.107
  196.7 0.7 slice.106
  197.5 1.9 multiply_cosine_fusion
  199.4 1.1 copy.80
  200.4 0.8 copy.81
  201.2 131.7 %all-gather.11.cloned.1.call-done = bf16[2560,512]{1,0:T(8,128)(2,1)} async-done(((bf16[40,512]{1,0:T(8,128)(2,1)}), bf16[2560,512]{1,0:T(8,128)(2,1)}) %all-gather.11.cloned.1.call-update) | async-done | bytes 2621456 | tf_op jit(solution)/shard_map/all_gather | solution.py:173
  332.9 3.3 fusion.4
  337.4 0.6 fusion.59
  338.0 33.0 %all-gather.7.cloned.1.call-done = bf16[32,2,128,256]{3,2,1,0:T(8,128)(2,1)} async-done(((bf16[4,2,128,256]{3,2,1,0:T(8,128)(2,1)}), bf16[32,2,128,256]{3,2,1,0:T(8,128)(2,1)}) %all-gather.7.cloned.1.call-update) | async-done | bytes 4194320 | tf_op jit(solution)/shard_map/all_gather | solution.py:190
  371.0 5.1 gather_fusion
  376.1 2.7 copy_select_fusion
  378.8 0.5 fusion.56
  379.3 1.0 fusion.6
  380.4 0.7 fusion.7
  381.6 0.9 fusion.9
  382.5 0.5 copy.88
  383.1 131.6 %all-gather.15.cloned.1.call-done = bf16[512,2560]{0,1:T(8,128)(2,1)} async-done(((bf16[512,40]{0,1:T(8,128)(2,1)}), bf16[512,2560]{0,1:T(8,128)(2,1)}) %all-gather.15.cloned.1.call-update) | async-done | bytes 2621456 | tf_op jit(solution)/shard_map/all_gather | solution.py:119
  514.8 4.8 convolution_convert_fusion
  519.6 3.0 copy.91
  522.6 2.9 reshape.548
  525.5 4.6 copy.92
  530.1 6.2 %reshape.549 = bf16[512,2560]{0,1:T(8,128)(2,1)} reshape(bf16[512,8,64,5]{0,3,2,1:T(8,128)(2,1)} %copy.92) | data formatting | bytes 5242880 | tf_op jit(solution)/shard_map/reshape | solution.py:124
  536.4 0.6 dynamic_slice.24
  537.0 0.6 dynamic_slice.22
  539.1 0.6 gather_fusion.3
  540.6 0.5 iota_subtract_fusion
  541.3 1.0 fusion.12
  542.9 0.6 gather_fusion.4
  543.5 0.9 broadcast_select_fusion
  544.4 31.1 %reduce-scatter.2.cloned.1.call-done = bf16[512,320]{0,1:T(8,128)(2,1)} async-done(((bf16[512,2560]{0,1:T(8,128)(2,1)}), bf16[512,320]{0,1:T(8,128)(2,1)}) %reduce-scatter.2.cloned.1.call-update) | async-done | bytes 327696 | tf_op jit(solution)/shard_map/reduce_scatter | solution.py:128
  (94 shorter events, 5.6 us)
Async XLA Ops:
  7.2 19.6 %copy-start.12 = (s32[8,64]{1,0:T(8,128)S(1)}, s32[8,64]{1,0:T(8,128)}, u32[]{:S(2)}) copy-start(s32[8,64]{1,0:T(8,128)} %param.17) | copy-start | bytes 6148
  7.2 41.1 %all-gather.9.cloned.1.call-start = ((), (), s32[]{:S(2)}) async-start(), calls=%async_computation.2 | async-start | bytes 2949120 | tf_op jit(solution)/shard_map/all_gather | solution.py:156
  7.9 184.8 %all-gather.13.cloned.1.call-start = ((), (), s32[]{:S(2)}) async-start(), calls=%async_computation.4 | async-start | bytes 2662400 | tf_op jit(solution)/shard_map/all_gather | solution.py:95
  8.7 324.3 %all-gather.11.cloned.1.call-start = ((), (), s32[]{:S(2)}) async-start(), calls=%async_computation.3 | async-start | bytes 2662400 | tf_op jit(solution)/shard_map/all_gather | solution.py:173
  11.1 359.9 %all-gather.7.cloned.1.call-start = ((), (), s32[]{:S(2)}) async-start(), calls=%async_computation.1 | async-start | bytes 4718592 | tf_op jit(solution)/shard_map/all_gather | solution.py:190
  11.7 503.1 %all-gather.15.cloned.1.call-start = ((), (), s32[]{:S(2)}) async-start(), calls=%async_computation.5 | async-start | bytes 2662400 | tf_op jit(solution)/shard_map/all_gather | solution.py:119
  25.5 3.9 copy-start.9
  25.5 4.9 copy-start.8
  26.7 548.7 %reduce-scatter.2.cloned.1.call-start = ((), (), s32[]{:S(2)}) async-start(), calls=%async_computation.6 | async-start | bytes 2949120 | tf_op jit(solution)/shard_map/reduce_scatter | solution.py:128
  48.3 144.5 %copy-start = (bf16[512,2560]{0,1:T(8,128)(2,1)S(1)}, bf16[512,2560]{0,1:T(8,128)(2,1)}, u32[]{:S(2)}) copy-start(bf16[512,2560]{0,1:T(8,128)(2,1)} %all-gather.9.cloned.1.call-done) | copy-start | bytes 7864324
  50.8 145.2 %copy-start.10 = (f32[512]{0:T(512)}, f32[512]{0:T(512)S(1)}, u32[]{:S(2)}) copy-start(f32[512]{0:T(512)S(1)} %add_rsqrt_fusion) | copy-start | bytes 6148
  201.2 135.1 %copy-start.2 = (f32[512,64]{0,1:T(8,128)S(1)}, f32[512,64]{0,1:T(8,128)}, u32[]{:S(2)}) copy-start(f32[512,64]{0,1:T(8,128)} %copy.81) | copy-start | bytes 393220
  336.4 1.0 copy-start.3
  336.4 1.0 copy-start.4
  336.4 1.0 copy-start.5
  336.4 1.0 copy-start.7
  338.0 38.1 %copy-start.11 = (pred[8,4]{1,0:T(8,128)(4,1)S(1)}, pred[8,4]{1,0:T(8,128)(4,1)}, u32[]{:S(2)}) copy-start(pred[8,4]{1,0:T(8,128)(4,1)} %copy.75) | copy-start | bytes 100
  380.3 1.0 copy-start.6
  536.3 0.7 copy-start.13
  536.3 2.8 copy-start.1
Sparse Core Ops, SparseCore 0:
  10.1 38.1 all-gather.8
  51.2 141.4 all-gather.12
  195.7 137.1 all-gather.10
  334.9 36.0 all-gather.6
  373.8 140.8 all-gather.14
  536.5 38.9 reduce-scatter.1
where the time goes:
time: 583 us; the launch traced here: 582 us
  waiting for transfers between devices  488 us (84%)
  local copies, waits for them, and re-layouts  33.8 us (6%)
  matrix products  18.1 us (3%)
  between operations  16.5 us (3%)
  blocking collectives  13.6 us (2%)
  other arithmetic  12 us (2%)
    all_gather x1, waiting for transfers between devices, project_memory(): lax.all_gather(keyvalue_weight, 'tok', axis=0, tiled=True)  142 us
    all_gather x1, waiting for transfers between devices, shards(): lax.all_gather(my_query_weight, 'tok', axis=0, tiled=True)  132 us
    all_gather x1, waiting for transfers between devices, reduce_heads(): lax.all_gather(my_output_weight, 'tok', axis=1, tiled=True)  132 us
    all_gather x1, waiting for transfers between devices, shards(): page_pool = lax.all_gather(cache, 'head', axis=0, tiled=True)  33 us
    reduce_scatter x1, waiting for transfers between devices, reduce_heads(): lax.psum_scatter(partial_value.astype(jnp.float32).astype(jnp.bfloat16),...  31.1 us
    all_gather x1, waiting for transfers between devices, shards(): gathered = lax.all_gather(tokens, 'head', axis=1, tiled=True)  16.7 us
    all_gather x1, blocking collectives, reduce_heads(): blocks = lax.all_gather(output_weight, 'head', axis=1, tiled=True)  13.6 us
  transfers between devices with their start and end apart: 6, of which 6 were waited for; matrix products, arithmetic and copies ran while one was open for 7% of the time, Pallas kernels for 0%

commit v1 on v0

--- a/solution.py
+++ b/solution.py
@@ -10,6 +10,24 @@
 PAGE = 128
 NPR = 4
 WINDOW = 256
+
+
+def ring_gather(array, axis, dim):
+    ways, here, step = (lax.axis_size(axis), lax.axis_index(axis), array.shape[dim])
+    shape = [n * ways if d == dim else n for d, n in enumerate(array.shape)]
+    full = lax.dynamic_update_slice_in_dim(
+        jnp.zeros(shape, array.dtype), array, here * step, axis=dim
+    )
+    going_up = going_down = array
+    for far in range(1, ways // 2 + 1):
+        going_up = lax.ppermute(going_up, axis, [(d, (d + 1) % ways) for d in range(ways)])
+        full = lax.dynamic_update_slice_in_dim(full, going_up, (here - far) % ways * step, axis=dim)
+        if 2 * far < ways:
+            going_down = lax.ppermute(going_down, axis, [(d, (d - 1) % ways) for d in range(ways)])
+            full = lax.dynamic_update_slice_in_dim(
+                full, going_down, (here + far) % ways * step, axis=dim
+            )
+    return full
 
 
 def ancestry(parent_row):
@@ -153,7 +171,7 @@
     owned = requests // head_count
     rows_owned = owned * DRAFT
     pages_dev = cache.shape[0]
-    gathered = lax.all_gather(tokens, "head", axis=1, tiled=True)
+    gathered = ring_gather(tokens, "head", 1)
     wide = gathered.astype(jnp.float32)
     mean_square = jnp.mean(wide * wide, axis=1, keepdims=True)
     normed = (wide * lax.rsqrt(mean_square + 1e-06)).astype(jnp.bfloat16)

time: 583 us -> 547 us (0.938)
  waiting for transfers between devices: 488 us -> 442 us
  starting transfers between devices: 0.24 us -> 9.11 us
    all_gather x1, waiting for transfers between devices: 142 us -> 98.2 us  [project_memory(): lax.all_gather(keyvalue_weight, 'tok', axis=0, tiled=True)]
    all_gather x1 -> x0, waiting for transfers between devices: 16.7 us -> none  [shards(): gathered = lax.all_gather(tokens, 'head', axis=1, tiled=True)]
    ppermute x0 -> x7, waiting for transfers between devices: none -> 15 us  [the longest x4 13.2 us: ring_gather(): lax.ppermute(going_up, axis, [(d, (d + 1) % ways) for d in range(ways)])]
    ppermute x0 -> x7, starting transfers between devices: none -> 8.91 us  [the longest x3 8.53 us: ring_gather(): lax.ppermute(going_down, axis, [(d, (d - 1) % ways) for d in range(ways)])]
  transfers between devices with their start and end apart: 6 -> 12, of which waited for: 6 -> 9; matrix products, arithmetic and copies ran while one was open for 7% -> 8% of each run, Pallas kernels for 0% -> 0%
where the time goes in v1:
time: 547 us; the launch traced here: 546 us
  waiting for transfers between devices  442 us (81%)
  local copies, waits for them, and re-layouts  36.2 us (7%)
  matrix products  18.1 us (3%)
  between operations  16.5 us (3%)
  blocking collectives  13.6 us (2%)
  other arithmetic  10.2 us (2%)
  starting transfers between devices  9.11 us (2%)
    all_gather x1, waiting for transfers between devices, shards(): lax.all_gather(my_query_weight, 'tok', axis=0, tiled=True)  132 us
    all_gather x1, waiting for transfers between devices, reduce_heads(): lax.all_gather(my_output_weight, 'tok', axis=1, tiled=True)  132 us
    all_gather x1, waiting for transfers between devices, project_memory(): lax.all_gather(keyvalue_weight, 'tok', axis=0, tiled=True)  98.2 us
    all_gather x1, waiting for transfers between devices, shards(): page_pool = lax.all_gather(cache, 'head', axis=0, tiled=True)  33.2 us
    reduce_scatter x1, waiting for transfers between devices, reduce_heads(): lax.psum_scatter(partial_value.astype(jnp.float32).astype(jnp.bfloat16),...  31 us
    all_gather x1, blocking collectives, reduce_heads(): blocks = lax.all_gather(output_weight, 'head', axis=1, tiled=True)  13.6 us
    ppermute x4, waiting for transfers between devices, ring_gather(): lax.ppermute(going_up, axis, [(d, (d + 1) % ways) for d in range(ways)])  13.2 us
  transfers between devices with their start and end apart: 12, of which 9 were waited for; matrix products, arithmetic and copies ran while one was open for 8% of the time, Pallas kernels for 0%

profile of v1, /device:TPU:2, one launch (start us, length us, event | category | flops | bytes accessed | tf_op | source)
XLA Modules:
  0.0 545.8 jit_solution(7027074084581715614)
XLA Ops:
  7.2 0.7 all-gather.10.cloned.1.call-update
  8.1 0.9 copy.116
  9.7 0.6 select_multiply_fusion.1
  10.4 0.7 all-gather.6.cloned.1.call-update
  11.2 2.9 collective-permute-start.1
  14.1 13.6 %all-gather = bf16[8,5,2560]{2,1,0:T(8,128)(2,1)S(1)} all-gather(bf16[1,5,2560]{2,1,0:T(8,128)(2,1)} %bitcast.138), channel_id=1, replica_groups=mesh['tok'=64,'head'=8] {'head'}, dimensions={0}, use_global_device_ids=true | all-gather | bytes 230400 | tf_op jit(solution)/shard_map/all_gather | solution.py:129
  28.4 0.6 select_multiply_fusion
  32.2 0.7 copy.75
  33.0 0.8 copy.86
  34.7 2.6 collective-permute-start.3
  37.3 4.7 collective-permute-done.2
  42.0 1.0 constant_dynamic-update-slice_fusion.6
  43.0 1.0 constant_dynamic-update-slice_fusion.5
  44.0 3.0 collective-permute-start.5
  47.0 2.7 collective-permute-done.4
  49.7 1.8 collective-permute-done.5
  51.6 5.8 %collective-permute-done.6 = bf16[512,320]{0,1:T(8,128)(2,1)S(1)} collective-permute-done((bf16[512,320]{0,1:T(8,128)(2,1)S(1)}, bf16[512,320]{0,1:T(8,128)(2,1)S(1)}, u32[]{:S(2)}, u32[]{:S(2)}) %collective-permute-start.6) | collective-permute-done | bytes 327712 | tf_op jit(solution)/shard_map/ppermute | solution.py:23
  57.4 0.6 fusion
  58.1 98.2 %all-gather.10.cloned.1.call-done = bf16[2560,512]{1,0:T(8,128)(2,1)} async-done(((bf16[40,512]{1,0:T(8,128)(2,1)}), bf16[2560,512]{1,0:T(8,128)(2,1)}) %all-gather.10.cloned.1.call-update) | async-done | bytes 2621456 | tf_op jit(solution)/shard_map/all_gather | solution.py:113
  156.3 3.3 fusion.2
  159.6 0.7 slice.107
  160.3 0.7 slice.106
  161.0 1.9 multiply_cosine_fusion
  162.9 1.1 copy.80
  164.0 0.8 copy.81
  164.7 131.7 %all-gather.8.cloned.1.call-done = bf16[2560,512]{1,0:T(8,128)(2,1)} async-done(((bf16[40,512]{1,0:T(8,128)(2,1)}), bf16[2560,512]{1,0:T(8,128)(2,1)}) %all-gather.8.cloned.1.call-update) | async-done | bytes 2621456 | tf_op jit(solution)/shard_map/all_gather | solution.py:191
  296.5 3.3 fusion.4
  301.0 0.6 fusion.61
  301.6 33.2 %all-gather.6.cloned.1.call-done = bf16[32,2,128,256]{3,2,1,0:T(8,128)(2,1)} async-done(((bf16[4,2,128,256]{3,2,1,0:T(8,128)(2,1)}), bf16[32,2,128,256]{3,2,1,0:T(8,128)(2,1)}) %all-gather.6.cloned.1.call-update) | async-done | bytes 4194320 | tf_op jit(solution)/shard_map/all_gather | solution.py:208
  334.7 5.1 gather_fusion
  339.8 2.7 copy_select_fusion
  343.0 1.0 fusion.6
  344.1 0.7 fusion.7
  345.3 0.9 fusion.9
  346.8 131.6 %all-gather.12.cloned.1.call-done = bf16[512,2560]{0,1:T(8,128)(2,1)} async-done(((bf16[512,40]{0,1:T(8,128)(2,1)}), bf16[512,2560]{0,1:T(8,128)(2,1)}) %all-gather.12.cloned.1.call-update) | async-done | bytes 2621456 | tf_op jit(solution)/shard_map/all_gather | solution.py:137
  478.5 4.8 convolution_convert_fusion
  483.3 3.0 copy.91
  486.3 2.9 reshape.548
  489.2 4.7 copy.92
  493.8 6.2 %reshape.549 = bf16[512,2560]{0,1:T(8,128)(2,1)} reshape(bf16[512,8,64,5]{0,3,2,1:T(8,128)(2,1)} %copy.92) | data formatting | bytes 5242880 | tf_op jit(solution)/shard_map/reshape | solution.py:142
  500.1 0.6 dynamic_slice.24
  500.7 0.6 dynamic_slice.22
  502.9 0.6 gather_fusion.3
  504.4 0.6 iota_subtract_fusion
  505.1 1.0 fusion.12
  506.8 0.6 gather_fusion.4
  507.4 0.9 broadcast_select_fusion
  508.3 31.0 %reduce-scatter.2.cloned.1.call-done = bf16[512,320]{0,1:T(8,128)(2,1)} async-done(((bf16[512,2560]{0,1:T(8,128)(2,1)}), bf16[512,320]{0,1:T(8,128)(2,1)}) %reduce-scatter.2.cloned.1.call-update) | async-done | bytes 327696 | tf_op jit(solution)/shard_map/reduce_scatter | solution.py:146
  (114 shorter events, 9.7 us)
Async XLA Ops:
  7.2 22.0 %copy-start.12 = (s32[8,64]{1,0:T(8,128)S(1)}, s32[8,64]{1,0:T(8,128)}, u32[]{:S(2)}) copy-start(s32[8,64]{1,0:T(8,128)} %param.17) | copy-start | bytes 6148
  7.2 149.1 %all-gather.10.cloned.1.call-start = ((), (), s32[]{:S(2)}) async-start(), calls=%async_computation.3 | async-start | bytes 2662400 | tf_op jit(solution)/shard_map/all_gather | solution.py:113
  7.9 288.6 %all-gather.8.cloned.1.call-start = ((), (), s32[]{:S(2)}) async-start(), calls=%async_computation.2 | async-start | bytes 2662400 | tf_op jit(solution)/shard_map/all_gather | solution.py:191
  10.3 324.4 %all-gather.6.cloned.1.call-start = ((), (), s32[]{:S(2)}) async-start(), calls=%async_computation.1 | async-start | bytes 4718592 | tf_op jit(solution)/shard_map/all_gather | solution.py:208
  11.1 467.4 %all-gather.12.cloned.1.call-start = ((), (), s32[]{:S(2)}) async-start(), calls=%async_computation.4 | async-start | bytes 2662400 | tf_op jit(solution)/shard_map/all_gather | solution.py:137
  11.1 22.9 %collective-permute-start = (bf16[512,320]{0,1:T(8,128)(2,1)}, bf16[512,320]{0,1:T(8,128)(2,1)}, u32[]{:S(2)}, u32[]{:S(2)}) collective-permute-start(bf16[512,320]{0,1:T(8,128)(2,1)} %param.11), channel_id=1, source_target_pairs={{0,1},{1,2},{2,3},{3,4},{4,5},{5,6},{6,7},{7,0},{8,9},{9,10},{10,1... | collective-permute-start | bytes 983048 | tf_op jit(solution)/shard_map/ppermute | solution.py:23
  11.2 23.5 %collective-permute-start.1 = (bf16[512,320]{0,1:T(8,128)(2,1)}, bf16[512,320]{0,1:T(8,128)(2,1)}, u32[]{:S(2)}, u32[]{:S(2)}) collective-permute-start(bf16[512,320]{0,1:T(8,128)(2,1)} %param.11), channel_id=1, source_target_pairs={{0,7},{1,0},{2,1},{3,2},{4,3},{5,4},{6,5},{7,6},{8,15},{9,8},{10,9... | collective-permute-start | bytes 983048 | tf_op jit(solution)/shard_map/ppermute | solution.py:26
  27.7 4.1 copy-start.9
  27.8 4.3 copy-start.8
  29.0 510.2 %reduce-scatter.2.cloned.1.call-start = ((), (), s32[]{:S(2)}) async-start(), calls=%async_computation.5 | async-start | bytes 2949120 | tf_op jit(solution)/shard_map/reduce_scatter | solution.py:146
  30.5 3.4 copy-start.6
  34.0 7.9 %collective-permute-start.2 = (bf16[512,320]{0,1:T(8,128)(2,1)}, bf16[512,320]{0,1:T(8,128)(2,1)S(1)}, u32[]{:S(2)}, u32[]{:S(2)}) collective-permute-start(bf16[512,320]{0,1:T(8,128)(2,1)} %collective-permute-done), channel_id=1, source_target_pairs={{0,1},{1,2},{2,3},{3,4},{4,5},{5,6},{6,7},{7,0},{8,9},{9,10},{10,1... | collective-permute-start | bytes 983048 | tf_op jit(solution)/shard_map/ppermute | solution.py:23
  34.7 9.3 %collective-permute-start.3 = (bf16[512,320]{0,1:T(8,128)(2,1)}, bf16[512,320]{0,1:T(8,128)(2,1)S(1)}, u32[]{:S(2)}, u32[]{:S(2)}) collective-permute-start(bf16[512,320]{0,1:T(8,128)(2,1)} %collective-permute-done.1), channel_id=1, source_target_pairs={{0,7},{1,0},{2,1},{3,2},{4,3},{5,4},{6,5},{7,6},{8,15},{9,8},{10,9... | collective-permute-start | bytes 983048 | tf_op jit(solution)/shard_map/ppermute | solution.py:26
  42.0 7.7 %collective-permute-start.4 = (bf16[512,320]{0,1:T(8,128)(2,1)S(1)}, bf16[512,320]{0,1:T(8,128)(2,1)S(1)}, u32[]{:S(2)}, u32[]{:S(2)}) collective-permute-start(bf16[512,320]{0,1:T(8,128)(2,1)S(1)} %collective-permute-done.2), channel_id=1, source_target_pairs={{0,1},{1,2},{2,3},{3,4},{4,5},{5,6},{6,7},{7,0},{8,9},{9,10},{10,1... | collective-permute-start | bytes 983048 | tf_op jit(solution)/shard_map/ppermute | solution.py:23
  44.0 7.6 %collective-permute-start.5 = (bf16[512,320]{0,1:T(8,128)(2,1)S(1)}, bf16[512,320]{0,1:T(8,128)(2,1)S(1)}, u32[]{:S(2)}, u32[]{:S(2)}) collective-permute-start(bf16[512,320]{0,1:T(8,128)(2,1)S(1)} %collective-permute-done.3), channel_id=1, source_target_pairs={{0,7},{1,0},{2,1},{3,2},{4,3},{5,4},{6,5},{7,6},{8,15},{9,8},{10,9... | collective-permute-start | bytes 983048 | tf_op jit(solution)/shard_map/ppermute | solution.py:26
  49.7 7.7 %collective-permute-start.6 = (bf16[512,320]{0,1:T(8,128)(2,1)S(1)}, bf16[512,320]{0,1:T(8,128)(2,1)S(1)}, u32[]{:S(2)}, u32[]{:S(2)}) collective-permute-start(bf16[512,320]{0,1:T(8,128)(2,1)S(1)} %collective-permute-done.4), channel_id=1, source_target_pairs={{0,1},{1,2},{2,3},{3,4},{4,5},{5,6},{6,7},{7,0},{8,9},{9,10},{10,1... | collective-permute-start | bytes 983048 | tf_op jit(solution)/shard_map/ppermute | solution.py:23
  58.0 101.5 %copy-start.10 = (f32[512]{0:T(512)}, f32[512]{0:T(512)S(1)}, u32[]{:S(2)}) copy-start(f32[512]{0:T(512)S(1)} %add_rsqrt_fusion) | copy-start | bytes 6148
  164.7 135.1 %copy-start.1 = (f32[512,64]{0,1:T(8,128)S(1)}, f32[512,64]{0,1:T(8,128)}, u32[]{:S(2)}) copy-start(f32[512,64]{0,1:T(8,128)} %copy.81) | copy-start | bytes 393220
  299.9 1.0 copy-start.2
  299.9 1.0 copy-start.3
  300.0 1.0 copy-start.4
  300.0 1.0 copy-start.7
  301.6 38.3 %copy-start.11 = (pred[8,4]{1,0:T(8,128)(4,1)S(1)}, pred[8,4]{1,0:T(8,128)(4,1)}, u32[]{:S(2)}) copy-start(pred[8,4]{1,0:T(8,128)(4,1)} %copy.75) | copy-start | bytes 100
  344.0 1.0 copy-start.5
  500.0 0.7 copy-start.13
  500.0 2.9 copy-start
Sparse Core Ops, SparseCore 0:
  10.9 145.3 all-gather.9
  159.2 137.1 all-gather.7
  298.6 36.0 all-gather.5
  337.5 140.8 all-gather.11
  500.2 38.9 reduce-scatter.1
